TPU v7x, 32 devices: a whole 2x2x4 slice. The times are simulated.
32 devices in a mesh: blk: 8 (over z, core), help: 4 (over y, x).
Axes of the slice: x: 2, y: 2, z: 4, core: 2. Of those that a mesh axis runs over, the one named last changes fastest.
Arguments:
- vectors: float32 [8, 16384], P(None, ('blk', 'help')), may hold values from -6 to 6
- tile_blocks: float32 [32, 5, 3, 256, 256], P(('blk', 'help')), may hold values from -0.1875 to 0.1875
- tile_row: int32 [32, 5, 3], P(('blk', 'help')), may hold values from 0 to 7
- tile_col: int32 [32, 5, 3], P(('blk', 'help')), may hold values from 0 to 7
- counts: int32 [32, 5], P(('blk', 'help')), may hold values from 1 to 3, as said below
Outputs:
- product: float32 [8, 16384], P(None, ('blk', 'help'))
- gram_energy: float32 [8, 8], replicated
- gram_correlation: float32 [8, 8], replicated
Inputs may be any that keep to these rules, and one draw needn't show every extreme that they name: `counts`: in every group of 4 helpers one helper has 3 live slots for every band offset; every other helper has fewer, and at least one, for each offset.
All inputs are finite; a program needn't handle non-finite values.
Results may differ from a plain program's by a relative error of at most 0.0003.
Values sent between devices are 32-bit elements; how exact they have to be, the bound alone decides.
No kernel may reach another device: no remote copies, remote signals or barrier semaphores. Data moves between devices by JAX's collectives and lax.ppermute only.
A program may use at most 64 MiB of HBM per device.

v0:
```python
import jax
import jax.numpy as jnp
from jax import lax
from jax.sharding import PartitionSpec as P

VEC = 8
TILE = 256
BAND = 2
SLOTS = 3
NOFF = 5


def shifted(value, axis, steps):
    count = lax.axis_size(axis)
    initial, last = (max(0, -steps), min(count, count - steps))
    return lax.ppermute(value, axis, [(source, source + steps) for source in range(initial, last)])


def neighbour_panels(source):
    lowers = []
    uppers = []
    current = source
    for hop_index in range(BAND):
        current = shifted(current, "blk", 1)
        lowers.append(current)
    current = source
    for hop_index in range(BAND):
        current = shifted(current, "blk", -1)
        uppers.append(current)
    return lowers[::-1] + [source] + uppers


def local(vectors, tile_blocks, tile_row, tile_col, counts):
    groups = lax.axis_size("blk")
    piece_width = vectors.shape[1]
    group_width = piece_width * lax.axis_size("help")
    group_rows = group_width // TILE
    full_panel = lax.all_gather(vectors, "help", axis=1, tiled=True)
    panels = neighbour_panels(full_panel)
    slot_ids = jnp.arange(SLOTS, dtype=jnp.int32)
    row_ids = jnp.arange(group_rows, dtype=jnp.int32)
    partial_value = jnp.zeros((VEC, group_rows, TILE), jnp.float32)
    for offset_index in range(NOFF):
        panel_tiles = panels[offset_index].reshape(VEC, group_rows, TILE)
        pieces = jnp.take(panel_tiles, tile_col[0, offset_index], axis=1)
        live = (slot_ids < counts[0, offset_index]).astype(jnp.float32)
        contribution = jnp.einsum(
            "ist,stu->isu", pieces, tile_blocks[0, offset_index], precision=lax.Precision.HIGHEST
        )
        one_hot = (tile_row[0, offset_index][:, None] == row_ids[None, :]).astype(
            jnp.float32
        ) * live[:, None]
        partial_value = partial_value + jnp.einsum(
            "isu,sr->iru", contribution, one_hot, precision=lax.Precision.HIGHEST
        )
    flattened = partial_value.reshape(VEC, group_width)
    basis_size = float(groups * group_width)
    correlation_term = jnp.dot(
        vectors, vectors.T, precision=lax.Precision.HIGHEST, preferred_element_type=jnp.float32
    )
    own_panel = panels[BAND]
    early_terms = (
        jnp.dot(
            own_panel,
            flattened.T,
            precision=lax.Precision.HIGHEST,
            preferred_element_type=jnp.float32,
        ),
        correlation_term,
    )
    gram_energy, gram_correlation = lax.psum((early_terms[0], early_terms[1]), ("blk", "help"))
    product = lax.psum_scatter(flattened, "help", scatter_dimension=1, tiled=True)
    return (product, gram_energy / basis_size, gram_correlation / basis_size)


def solution(mesh):
    placed = (
        P(None, ("blk", "help")),
        P(("blk", "help"), None, None, None, None),
        P(("blk", "help"), None, None),
        P(("blk", "help"), None, None),
        P(("blk", "help"), None),
    )
    return jax.shard_map(
        local,
        mesh=mesh,
        in_specs=placed,
        out_specs=(P(None, ("blk", "help")), P(), P()),
        check_vma=False,
    )
```

profile of v0, /device:TPU:0, one launch (start us, length us, event | category | flops | bytes accessed | tf_op | source)
XLA Modules:
  0.0 99.4 jit_solution(237913537589706720)
XLA Ops:
  7.2 0.0 reduce-scatter.2.cloned.1.call-start
  7.2 9.8 %all_gather.3 = f32[8,2048]{1,0:T(8,128)S(1)} all-gather(f32[8,512]{1,0:T(8,128)} %param.7), channel_id=1, replica_groups=mesh['blk'=8,'help'=4] {'help'}, dimensions={1}, use_global_device_ids=true | all-gather | bytes 81920 | tf_op jit(solution)/shard_map/all_gather | solution.py:38
  17.1 1.3 %collective-permute-start = (f32[8,2048]{1,0:T(8,128)S(1)}, f32[8,2048]{1,0:T(8,128)S(1)}, u32[]{:S(2)}, u32[]{:S(2)}) collective-permute-start(f32[8,2048]{1,0:T(8,128)S(1)} %all_gather.3), channel_id=1, source_target_pairs={{0,4},{4,8},{8,12},{12,16},{16,20},{20,24},{24,28},{1,5},{5,9},{9,... | collective-permute-start | bytes 196616 | tf_op jit(solution)/shard_map/ppermute | solution.py:16
  18.3 1.3 %collective-permute-start.2 = (f32[8,2048]{1,0:T(8,128)S(1)}, f32[8,2048]{1,0:T(8,128)S(1)}, u32[]{:S(2)}, u32[]{:S(2)}) collective-permute-start(f32[8,2048]{1,0:T(8,128)S(1)} %all_gather.3), channel_id=1, source_target_pairs={{4,0},{8,4},{12,8},{16,12},{20,16},{24,20},{28,24},{5,1},{9,5},{13... | collective-permute-start | bytes 196616 | tf_op jit(solution)/shard_map/ppermute | solution.py:16
  19.6 1.3 %slice_reduce_fusion = (s32[3]{0:T(128)S(1)}, s32[3]{0:T(128)S(1)}, s32[3]{0:T(128)S(1)}, s32[3]{0:T(128)S(1)}, s32[3]{0:T(128)S(1)}) fusion(s32[1,5,3]{1,0,2:T(1,128)} %param.10), kind=kLoop, calls=%fused_computation.94 | loop fusion | bytes 120 | tf_op jit(solution)/shard_map/slice | solution.py:45
  21.1 0.9 fusion.83
  22.0 1.4 %fusion.82 = (s32[1,1]{1,0:T(1,128)}, s32[1,1]{1,0:T(1,128)}, s32[1,1]{1,0:T(1,128)}, s32[1,1]{1,0:T(1,128)}, s32[1,1]{1,0:T(1,128)}) fusion(s32[1,5]{1,0:T(1,128)} %param.11), kind=kLoop, calls=%fused_computation.129 | loop fusion | bytes 40 | tf_op jit(solution)/shard_map/slice | solution.py:46
  23.5 0.7 compare_convert_fusion.4
  24.2 1.3 %slice_reduce_fusion.1 = (s32[3]{0:T(128)S(1)}, s32[3]{0:T(128)S(1)}, s32[3]{0:T(128)S(1)}, s32[3]{0:T(128)S(1)}, s32[3]{0:T(128)S(1)}) fusion(s32[1,5,3]{1,0,2:T(1,128)} %param.9), kind=kLoop, calls=%fused_computation.95 | loop fusion | bytes 120 | tf_op jit(solution)/shard_map/slice | solution.py:50
  25.5 0.7 compare_convert_fusion.3
  26.2 0.7 compare_convert_fusion.2
  26.8 0.6 compare_convert_fusion.1
  27.4 0.6 gather_fusion.2
  28.0 1.6 %fusion.5 = f32[3,8,256]{2,1,0:T(8,128)S(1)} fusion(f32[1,5,3,256,256]{4,3,2,1,0:T(8,128)} %param.8, f32[3,8,256]{2,1,0:T(8,128)S(1)} %gather_fusion.2, pred[3]{0:T(512)(128)(4,1)S(1)} %compare_and_fusion.2), kind=kOutput, calls=%fused_computation.15 | convolution fusion | flops 18880512 | bytes 835587 | tf_op jit(solution)/shard_map/ist,stu->isu/dot_general | solution.py:47
  29.6 0.7 compare_convert_fusion
  30.2 0.0 collective-permute-done
  30.3 0.6 gather_fusion.1
  30.8 1.6 %fusion.7 = f32[3,8,256]{2,1,0:T(8,128)S(1)} fusion(f32[1,5,3,256,256]{4,3,2,1,0:T(8,128)} %param.8, f32[3,8,256]{2,1,0:T(8,128)S(1)} %gather_fusion.1, pred[3]{0:T(512)(128)(4,1)S(1)} %compare_and_fusion.3), kind=kOutput, calls=%fused_computation.17 | convolution fusion | flops 18880512 | bytes 835587 | tf_op jit(solution)/shard_map/ist,stu->isu/dot_general | solution.py:47
  32.4 0.0 collective-permute-done.2
  32.4 0.6 gather_fusion.3
  33.0 4.8 %collective-permute-start.1 = (f32[8,2048]{1,0:T(8,128)S(1)}, f32[8,2048]{1,0:T(8,128)S(1)}, u32[]{:S(2)}, u32[]{:S(2)}) collective-permute-start(f32[8,2048]{1,0:T(8,128)S(1)} %collective-permute-done), channel_id=1, source_target_pairs={{0,4},{4,8},{8,12},{12,16},{16,20},{20,24},{24,28},{1,5},{5,9},{9,... | collective-permute-start | bytes 196616 | tf_op jit(solution)/shard_map/ppermute | solution.py:16
  37.8 1.6 %fusion.3 = f32[3,8,256]{2,1,0:T(8,128)S(1)} fusion(f32[1,5,3,256,256]{4,3,2,1,0:T(8,128)} %param.8, f32[3,8,256]{2,1,0:T(8,128)S(1)} %gather_fusion.3, pred[3]{0:T(512)(128)(4,1)S(1)} %compare_and_fusion.1), kind=kOutput, calls=%fused_computation.13 | convolution fusion | flops 18880512 | bytes 835587 | tf_op jit(solution)/shard_map/ist,stu->isu/dot_general | solution.py:47
  39.4 1.3 %collective-permute-start.3 = (f32[8,2048]{1,0:T(8,128)S(1)}, f32[8,2048]{1,0:T(8,128)S(1)}, u32[]{:S(2)}, u32[]{:S(2)}) collective-permute-start(f32[8,2048]{1,0:T(8,128)S(1)} %collective-permute-done.2), channel_id=1, source_target_pairs={{4,0},{8,4},{12,8},{16,12},{20,16},{24,20},{28,24},{5,1},{9,5},{13... | collective-permute-start | bytes 196616 | tf_op jit(solution)/shard_map/ppermute | solution.py:16
  40.8 0.0 collective-permute-done.1
  40.8 0.6 gather_fusion
  41.3 1.6 %fusion.9 = f32[3,8,256]{2,1,0:T(8,128)S(1)} fusion(f32[1,5,3,256,256]{4,3,2,1,0:T(8,128)} %param.8, f32[3,8,256]{2,1,0:T(8,128)S(1)} %gather_fusion, pred[3]{0:T(512)(128)(4,1)S(1)} %compare_and_fusion.4), kind=kOutput, calls=%fused_computation.19 | convolution fusion | flops 18880512 | bytes 835587 | tf_op jit(solution)/shard_map/ist,stu->isu/dot_general | solution.py:47
  42.9 0.9 collective-permute-done.3
  43.8 0.5 gather_fusion.4
  44.4 1.6 %fusion.1 = f32[3,8,256]{2,1,0:T(8,128)S(1)} fusion(f32[1,5,3,256,256]{4,3,2,1,0:T(8,128)} %param.8, f32[3,8,256]{2,1,0:T(8,128)S(1)} %gather_fusion.4, pred[3]{0:T(512)(128)(4,1)S(1)} %compare_and_fusion), kind=kOutput, calls=%fused_computation.11 | convolution fusion | flops 18880512 | bytes 835587 | tf_op jit(solution)/shard_map/ist,stu->isu/dot_general | solution.py:47
  46.0 0.4 fusion.20
  46.4 0.3 convolution_add_fusion.3
  46.7 0.3 convolution_add_fusion.2
  47.0 0.3 convolution_add_fusion.1
  47.3 0.3 fusion
  47.7 0.6 copy.20
  48.3 0.0 reduce-scatter.2.cloned.1.call-update
  48.3 1.0 %convolution_bitcast_fusion = f32[8,8]{0,1:T(8,128)S(1)} fusion(f32[8,2048]{1,0:T(8,128)} %bitcast.81, f32[8,2048]{1,0:T(8,128)S(1)} %all_gather.3), kind=kOutput, calls=%fused_computation.10 | convolution fusion | flops 1572864 | bytes 131328 | tf_op jit(solution)/shard_map/dot_general | solution.py:63
  49.4 41.8 %all-reduce = (f32[8,8]{0,1:T(8,128)S(1)}, f32[8,8]{0,1:T(8,128)S(1)}) all-reduce(f32[8,8]{0,1:T(8,128)S(1)} %convolution_bitcast_fusion, f32[8,8]{0,1:T(8,128)S(1)} %fusion.83), channel_id=1, replica_groups=mesh['blk'=8,'help'=4] {'blk','help'}, use_global_device_ids=true, to_apply=%region_1.3 | all-reduce | flops 128 | bytes 1024 | tf_op jit(solution)/shard_map/psum | solution.py:71
  91.2 0.7 copy.12
  91.9 0.7 copy.13
  92.5 0.0 reduce-scatter.2.cloned.1.call-done
  (16 shorter events, 0.1 us)
Async XLA Ops:
  7.2 85.4 %reduce-scatter.2.cloned.1.call-start = ((), (), s32[]{:S(2)}) async-start(), calls=%async_computation.1 | async-start | bytes 81920 | tf_op jit(solution)/shard_map/reduce_scatter | solution.py:72
  17.1 13.2 %collective-permute-start = (f32[8,2048]{1,0:T(8,128)S(1)}, f32[8,2048]{1,0:T(8,128)S(1)}, u32[]{:S(2)}, u32[]{:S(2)}) collective-permute-start(f32[8,2048]{1,0:T(8,128)S(1)} %all_gather.3), channel_id=1, source_target_pairs={{0,4},{4,8},{8,12},{12,16},{16,20},{20,24},{24,28},{1,5},{5,9},{9,... | collective-permute-start | bytes 196616 | tf_op jit(solution)/shard_map/ppermute | solution.py:16
  18.3 14.1 %collective-permute-start.2 = (f32[8,2048]{1,0:T(8,128)S(1)}, f32[8,2048]{1,0:T(8,128)S(1)}, u32[]{:S(2)}, u32[]{:S(2)}) collective-permute-start(f32[8,2048]{1,0:T(8,128)S(1)} %all_gather.3), channel_id=1, source_target_pairs={{4,0},{8,4},{12,8},{16,12},{20,16},{24,20},{28,24},{5,1},{9,5},{13... | collective-permute-start | bytes 196616 | tf_op jit(solution)/shard_map/ppermute | solution.py:16
  33.0 7.8 %collective-permute-start.1 = (f32[8,2048]{1,0:T(8,128)S(1)}, f32[8,2048]{1,0:T(8,128)S(1)}, u32[]{:S(2)}, u32[]{:S(2)}) collective-permute-start(f32[8,2048]{1,0:T(8,128)S(1)} %collective-permute-done), channel_id=1, source_target_pairs={{0,4},{4,8},{8,12},{12,16},{16,20},{20,24},{24,28},{1,5},{5,9},{9,... | collective-permute-start | bytes 196616 | tf_op jit(solution)/shard_map/ppermute | solution.py:16
  39.4 4.4 %collective-permute-start.3 = (f32[8,2048]{1,0:T(8,128)S(1)}, f32[8,2048]{1,0:T(8,128)S(1)}, u32[]{:S(2)}, u32[]{:S(2)}) collective-permute-start(f32[8,2048]{1,0:T(8,128)S(1)} %collective-permute-done.2), channel_id=1, source_target_pairs={{4,0},{8,4},{12,8},{16,12},{20,16},{24,20},{28,24},{5,1},{9,5},{13... | collective-permute-start | bytes 196616 | tf_op jit(solution)/shard_map/ppermute | solution.py:16
Sparse Core Ops, SparseCore 0:
  48.5 25.5 reduce-scatter.1
where the time goes:
time: 100 us; the launch traced here: 99.4 us
  blocking collectives  51.7 us (52%)
  between operations  14.4 us (14%)
  matrix products  11.5 us (12%)
  starting transfers between devices  8.77 us (9%)
  local copies, waits for them, and re-layouts  8.77 us (9%)
  other arithmetic  3.34 us (3%)
    psum x1, blocking collectives, local(): lax.psum((early_terms[0], early_terms[1]), ('blk', 'help'))  41.8 us
    all_gather x1, blocking collectives, local(): full_panel = lax.all_gather(vectors, 'help', axis=1, tiled=True)  9.85 us
    ppermute x4, starting transfers between devices, shifted(): lax.ppermute(value, axis, [(source, source + steps) for source in range(i...  8.73 us
    dot_general x5, matrix products, local(): jnp.einsum('ist,stu->isu', pieces, tile_blocks[0, offset_index], precisio...  7.92 us
    convert_element_type x5, other arithmetic, local(): live = (slot_ids < counts[0, offset_index]).astype(jnp.float32)  3.23 us
    gather x5, local copies, waits for them, and re-layouts, local(): pieces = jnp.take(panel_tiles, tile_col[0, offset_index], axis=1)  2.77 us
  transfers between devices with their start and end apart: 5, of which 1 were waited for; matrix products, arithmetic and copies ran while one was open for 19% of the time, Pallas kernels for 0%

commit v1 on v0

--- a/solution.py
+++ b/solution.py
@@ -68,7 +68,9 @@
         ),
         correlation_term,
     )
-    gram_energy, gram_correlation = lax.psum((early_terms[0], early_terms[1]), ("blk", "help"))
+    gram_energy, gram_correlation = lax.psum(
+        lax.psum((early_terms[0], early_terms[1]), axis_name="help"), axis_name="blk"
+    )
     product = lax.psum_scatter(flattened, "help", scatter_dimension=1, tiled=True)
     return (product, gram_energy / basis_size, gram_correlation / basis_size)
 

time: 100 us -> 82.9 us (0.83)
  blocking collectives: 51.7 us -> 34.5 us
    psum x1 -> x2, blocking collectives: 41.8 us -> 24.6 us  [the longest x1 15.5 us: local(): lax.psum(lax.psum((early_terms[0], early_terms[1]), axis_name='help'), ax...]
  transfers between devices with their start and end apart: 5 -> 5, of which waited for: 1 -> 1; matrix products, arithmetic and copies ran while one was open for 19% -> 23% of each run, Pallas kernels for 0% -> 0%
where the time goes in v1:
time: 82.9 us; the launch traced here: 82.2 us
  blocking collectives  34.5 us (42%)
  between operations  14.4 us (17%)
  matrix products  11.5 us (14%)
  starting transfers between devices  8.77 us (11%)
  local copies, waits for them, and re-layouts  8.77 us (11%)
  other arithmetic  3.34 us (4%)
  waiting for transfers between devices  0.95 us (1%)
    psum x1, blocking collectives, local(): lax.psum(lax.psum((early_terms[0], early_terms[1]), axis_name='help'), ax...  15.5 us
    all_gather x1, blocking collectives, local(): full_panel = lax.all_gather(vectors, 'help', axis=1, tiled=True)  9.85 us
    psum x1, blocking collectives, local(): lax.psum((early_terms[0], early_terms[1]), axis_name='help')  9.12 us
    ppermute x4, starting transfers between devices, shifted(): lax.ppermute(value, axis, [(source, source + steps) for source in range(i...  8.73 us
    dot_general x5, matrix products, local(): jnp.einsum('ist,stu->isu', pieces, tile_blocks[0, offset_index], precisio...  7.92 us
    convert_element_type x5, other arithmetic, local(): live = (slot_ids < counts[0, offset_index]).astype(jnp.float32)  3.23 us
    gather x5, local copies, waits for them, and re-layouts, local(): pieces = jnp.take(panel_tiles, tile_col[0, offset_index], axis=1)  2.77 us
    unnamed x3, local copies, waits for them, and re-layouts  1.96 us
  transfers between devices with their start and end apart: 5, of which 1 were waited for; matrix products, arithmetic and copies ran while one was open for 23% of the time, Pallas kernels for 0%

profile of v1, /device:TPU:0, one launch (start us, length us, event | category | flops | bytes accessed | tf_op | source)
XLA Modules:
  0.0 82.2 jit_solution(9111987876331550953)
XLA Ops:
  7.2 0.0 reduce-scatter.2.cloned.1.call-start
  7.2 9.8 %all_gather.3 = f32[8,2048]{1,0:T(8,128)S(1)} all-gather(f32[8,512]{1,0:T(8,128)} %param.7), channel_id=1, replica_groups=mesh['blk'=8,'help'=4] {'help'}, dimensions={1}, use_global_device_ids=true | all-gather | bytes 81920 | tf_op jit(solution)/shard_map/all_gather | solution.py:38
  17.1 1.3 %collective-permute-start = (f32[8,2048]{1,0:T(8,128)S(1)}, f32[8,2048]{1,0:T(8,128)S(1)}, u32[]{:S(2)}, u32[]{:S(2)}) collective-permute-start(f32[8,2048]{1,0:T(8,128)S(1)} %all_gather.3), channel_id=1, source_target_pairs={{0,4},{4,8},{8,12},{12,16},{16,20},{20,24},{24,28},{1,5},{5,9},{9,... | collective-permute-start | bytes 196616 | tf_op jit(solution)/shard_map/ppermute | solution.py:16
  18.3 1.3 %collective-permute-start.2 = (f32[8,2048]{1,0:T(8,128)S(1)}, f32[8,2048]{1,0:T(8,128)S(1)}, u32[]{:S(2)}, u32[]{:S(2)}) collective-permute-start(f32[8,2048]{1,0:T(8,128)S(1)} %all_gather.3), channel_id=1, source_target_pairs={{4,0},{8,4},{12,8},{16,12},{20,16},{24,20},{28,24},{5,1},{9,5},{13... | collective-permute-start | bytes 196616 | tf_op jit(solution)/shard_map/ppermute | solution.py:16
  19.6 1.3 %slice_reduce_fusion = (s32[3]{0:T(128)S(1)}, s32[3]{0:T(128)S(1)}, s32[3]{0:T(128)S(1)}, s32[3]{0:T(128)S(1)}, s32[3]{0:T(128)S(1)}) fusion(s32[1,5,3]{1,0,2:T(1,128)} %param.10), kind=kLoop, calls=%fused_computation.94 | loop fusion | bytes 120 | tf_op jit(solution)/shard_map/slice | solution.py:45
  21.1 0.9 %fusion.83 = f32[8,8]{0,1:T(8,128)S(1)} fusion(f32[8,512]{1,0:T(8,128)} %param.7), kind=kOutput, calls=%fused_computation.130 | convolution fusion | flops 393216 | bytes 16640 | tf_op jit(solution)/shard_map/dot_general | solution.py:58
  22.0 1.4 %fusion.82 = (s32[1,1]{1,0:T(1,128)}, s32[1,1]{1,0:T(1,128)}, s32[1,1]{1,0:T(1,128)}, s32[1,1]{1,0:T(1,128)}, s32[1,1]{1,0:T(1,128)}) fusion(s32[1,5]{1,0:T(1,128)} %param.11), kind=kLoop, calls=%fused_computation.129 | loop fusion | bytes 40 | tf_op jit(solution)/shard_map/slice | solution.py:46
  23.5 0.7 compare_convert_fusion.4
  24.2 1.3 %slice_reduce_fusion.1 = (s32[3]{0:T(128)S(1)}, s32[3]{0:T(128)S(1)}, s32[3]{0:T(128)S(1)}, s32[3]{0:T(128)S(1)}, s32[3]{0:T(128)S(1)}) fusion(s32[1,5,3]{1,0,2:T(1,128)} %param.9), kind=kLoop, calls=%fused_computation.95 | loop fusion | bytes 120 | tf_op jit(solution)/shard_map/slice | solution.py:50
  25.5 0.7 compare_convert_fusion.3
  26.2 0.7 compare_convert_fusion.2
  26.8 0.6 compare_convert_fusion.1
  27.4 0.6 gather_fusion.2
  28.0 1.6 %fusion.5 = f32[3,8,256]{2,1,0:T(8,128)S(1)} fusion(f32[1,5,3,256,256]{4,3,2,1,0:T(8,128)} %param.8, f32[3,8,256]{2,1,0:T(8,128)S(1)} %gather_fusion.2, pred[3]{0:T(512)(128)(4,1)S(1)} %compare_and_fusion.2), kind=kOutput, calls=%fused_computation.15 | convolution fusion | flops 18880512 | bytes 835587 | tf_op jit(solution)/shard_map/ist,stu->isu/dot_general | solution.py:47
  29.6 0.7 compare_convert_fusion
  30.2 0.0 collective-permute-done
  30.3 0.6 gather_fusion.1
  30.8 1.6 %fusion.7 = f32[3,8,256]{2,1,0:T(8,128)S(1)} fusion(f32[1,5,3,256,256]{4,3,2,1,0:T(8,128)} %param.8, f32[3,8,256]{2,1,0:T(8,128)S(1)} %gather_fusion.1, pred[3]{0:T(512)(128)(4,1)S(1)} %compare_and_fusion.3), kind=kOutput, calls=%fused_computation.17 | convolution fusion | flops 18880512 | bytes 835587 | tf_op jit(solution)/shard_map/ist,stu->isu/dot_general | solution.py:47
  32.4 0.0 collective-permute-done.2
  32.4 0.6 gather_fusion.3
  33.0 4.8 %collective-permute-start.1 = (f32[8,2048]{1,0:T(8,128)S(1)}, f32[8,2048]{1,0:T(8,128)S(1)}, u32[]{:S(2)}, u32[]{:S(2)}) collective-permute-start(f32[8,2048]{1,0:T(8,128)S(1)} %collective-permute-done), channel_id=1, source_target_pairs={{0,4},{4,8},{8,12},{12,16},{16,20},{20,24},{24,28},{1,5},{5,9},{9,... | collective-permute-start | bytes 196616 | tf_op jit(solution)/shard_map/ppermute | solution.py:16
  37.8 1.6 %fusion.3 = f32[3,8,256]{2,1,0:T(8,128)S(1)} fusion(f32[1,5,3,256,256]{4,3,2,1,0:T(8,128)} %param.8, f32[3,8,256]{2,1,0:T(8,128)S(1)} %gather_fusion.3, pred[3]{0:T(512)(128)(4,1)S(1)} %compare_and_fusion.1), kind=kOutput, calls=%fused_computation.13 | convolution fusion | flops 18880512 | bytes 835587 | tf_op jit(solution)/shard_map/ist,stu->isu/dot_general | solution.py:47
  39.4 1.3 %collective-permute-start.3 = (f32[8,2048]{1,0:T(8,128)S(1)}, f32[8,2048]{1,0:T(8,128)S(1)}, u32[]{:S(2)}, u32[]{:S(2)}) collective-permute-start(f32[8,2048]{1,0:T(8,128)S(1)} %collective-permute-done.2), channel_id=1, source_target_pairs={{4,0},{8,4},{12,8},{16,12},{20,16},{24,20},{28,24},{5,1},{9,5},{13... | collective-permute-start | bytes 196616 | tf_op jit(solution)/shard_map/ppermute | solution.py:16
  40.8 0.0 collective-permute-done.1
  40.8 0.6 gather_fusion
  41.3 1.6 %fusion.9 = f32[3,8,256]{2,1,0:T(8,128)S(1)} fusion(f32[1,5,3,256,256]{4,3,2,1,0:T(8,128)} %param.8, f32[3,8,256]{2,1,0:T(8,128)S(1)} %gather_fusion, pred[3]{0:T(512)(128)(4,1)S(1)} %compare_and_fusion.4), kind=kOutput, calls=%fused_computation.19 | convolution fusion | flops 18880512 | bytes 835587 | tf_op jit(solution)/shard_map/ist,stu->isu/dot_general | solution.py:47
  42.9 0.9 %collective-permute-done.3 = f32[8,2048]{1,0:T(8,128)S(1)} collective-permute-done((f32[8,2048]{1,0:T(8,128)S(1)}, f32[8,2048]{1,0:T(8,128)S(1)}, u32[]{:S(2)}, u32[]{:S(2)}) %collective-permute-start.3) | collective-permute-done | bytes 65568 | tf_op jit(solution)/shard_map/ppermute | solution.py:16
  43.8 0.5 gather_fusion.4
  44.4 1.6 %fusion.1 = f32[3,8,256]{2,1,0:T(8,128)S(1)} fusion(f32[1,5,3,256,256]{4,3,2,1,0:T(8,128)} %param.8, f32[3,8,256]{2,1,0:T(8,128)S(1)} %gather_fusion.4, pred[3]{0:T(512)(128)(4,1)S(1)} %compare_and_fusion), kind=kOutput, calls=%fused_computation.11 | convolution fusion | flops 18880512 | bytes 835587 | tf_op jit(solution)/shard_map/ist,stu->isu/dot_general | solution.py:47
  46.0 0.4 fusion.20
  46.4 0.3 convolution_add_fusion.3
  46.7 0.3 convolution_add_fusion.2
  47.0 0.3 convolution_add_fusion.1
  47.3 0.3 fusion
  47.7 0.6 copy.20
  48.3 0.0 reduce-scatter.2.cloned.1.call-update
  48.3 1.0 %convolution_bitcast_fusion = f32[8,8]{0,1:T(8,128)S(1)} fusion(f32[8,2048]{1,0:T(8,128)} %bitcast.81, f32[8,2048]{1,0:T(8,128)S(1)} %all_gather.3), kind=kOutput, calls=%fused_computation.10 | convolution fusion | flops 1572864 | bytes 131328 | tf_op jit(solution)/shard_map/dot_general | solution.py:63
  49.4 9.1 %all-reduce.1 = (f32[8,8]{0,1:T(8,128)S(1)}, f32[8,8]{0,1:T(8,128)S(1)}) all-reduce(f32[8,8]{0,1:T(8,128)S(1)} %convolution_bitcast_fusion, f32[8,8]{0,1:T(8,128)S(1)} %fusion.83), channel_id=1, replica_groups=mesh['blk'=8,'help'=4] {'help'}, use_global_device_ids=true, to_apply=%region_1.3 | all-reduce | flops 128 | bytes 1024 | tf_op jit(solution)/shard_map/psum | solution.py:72
  58.5 15.5 %all-reduce = (f32[8,8]{0,1:T(8,128)S(1)}, f32[8,8]{0,1:T(8,128)S(1)}) all-reduce(f32[8,8]{0,1:T(8,128)S(1)} %get-tuple-element.22, f32[8,8]{0,1:T(8,128)S(1)} %get-tuple-element.23), channel_id=1, replica_groups=mesh['blk'=8,'help'=4] {'blk'}, use_global_device_ids=true, to_apply=%region_2.4 | all-reduce | flops 128 | bytes 1024 | tf_op jit(solution)/shard_map/psum | solution.py:71
  74.0 0.7 copy.12
  74.7 0.7 copy.13
  75.4 0.0 reduce-scatter.2.cloned.1.call-done
  (16 shorter events, 0.1 us)
Async XLA Ops:
  7.2 68.2 %reduce-scatter.2.cloned.1.call-start = ((), (), s32[]{:S(2)}) async-start(), calls=%async_computation.1 | async-start | bytes 81920 | tf_op jit(solution)/shard_map/reduce_scatter | solution.py:74
  17.1 13.2 %collective-permute-start = (f32[8,2048]{1,0:T(8,128)S(1)}, f32[8,2048]{1,0:T(8,128)S(1)}, u32[]{:S(2)}, u32[]{:S(2)}) collective-permute-start(f32[8,2048]{1,0:T(8,128)S(1)} %all_gather.3), channel_id=1, source_target_pairs={{0,4},{4,8},{8,12},{12,16},{16,20},{20,24},{24,28},{1,5},{5,9},{9,... | collective-permute-start | bytes 196616 | tf_op jit(solution)/shard_map/ppermute | solution.py:16
  18.3 14.1 %collective-permute-start.2 = (f32[8,2048]{1,0:T(8,128)S(1)}, f32[8,2048]{1,0:T(8,128)S(1)}, u32[]{:S(2)}, u32[]{:S(2)}) collective-permute-start(f32[8,2048]{1,0:T(8,128)S(1)} %all_gather.3), channel_id=1, source_target_pairs={{4,0},{8,4},{12,8},{16,12},{20,16},{24,20},{28,24},{5,1},{9,5},{13... | collective-permute-start | bytes 196616 | tf_op jit(solution)/shard_map/ppermute | solution.py:16
  33.0 7.8 %collective-permute-start.1 = (f32[8,2048]{1,0:T(8,128)S(1)}, f32[8,2048]{1,0:T(8,128)S(1)}, u32[]{:S(2)}, u32[]{:S(2)}) collective-permute-start(f32[8,2048]{1,0:T(8,128)S(1)} %collective-permute-done), channel_id=1, source_target_pairs={{0,4},{4,8},{8,12},{12,16},{16,20},{20,24},{24,28},{1,5},{5,9},{9,... | collective-permute-start | bytes 196616 | tf_op jit(solution)/shard_map/ppermute | solution.py:16
  39.4 4.4 %collective-permute-start.3 = (f32[8,2048]{1,0:T(8,128)S(1)}, f32[8,2048]{1,0:T(8,128)S(1)}, u32[]{:S(2)}, u32[]{:S(2)}) collective-permute-start(f32[8,2048]{1,0:T(8,128)S(1)} %collective-permute-done.2), channel_id=1, source_target_pairs={{4,0},{8,4},{12,8},{16,12},{20,16},{24,20},{28,24},{5,1},{9,5},{13... | collective-permute-start | bytes 196616 | tf_op jit(solution)/shard_map/ppermute | solution.py:16
Sparse Core Ops, SparseCore 0:
  48.5 25.5 reduce-scatter.1
